TPU v7x, 32 devices: a whole 2x2x4 slice. The times are simulated.
32 devices in a mesh: dp: 16 (over z, y, core), tensor: 2 (over x).
Axes of the slice: x: 2, y: 2, z: 4, core: 2. Of those that a mesh axis runs over, the one named last changes fastest.
Arguments:
- hidden_states: bfloat16 [8192, 2048], P('dp', 'tensor'), may hold values from -6 to 6
- norm_gain: bfloat16 [2048], replicated, may hold values from 0.25 to 1.75
- head_weight: bfloat16 [2048, 25600], P(None, ('tensor', 'dp')), may hold values from -1 to 1
- target_ids: int32 [8192], P('dp'), may hold values from 0 to 25599
- loss_mask: int32 [8192], P('dp'), may hold values from 0 to 1, as said below
- seq_lengths: int32 [16], replicated, may hold values from 1 to 4096, as said below
- slot_order: int32 [16], replicated, may hold values from 0 to 15, each once
Outputs:
- token_logprob: float32 [8192], P(('dp', 'tensor'))
- token_entropy: float32 [8192], P(('dp', 'tensor'))
- seq_mean_logprob: float32 [16], P('dp')
- seq_mean_entropy: float32 [16], P('dp')
Inputs may be any that keep to these rules, and one draw needn't show every extreme that they name: `seq_lengths`: sequences lie in packed order, one after another; their lengths sum to 8192; the longest has exactly 4096 tokens and some sequence has exactly 1 token. `slot_order`: each sequence appears once. `loss_mask`: some sequence of exactly 1 token has no scored row.
All inputs are finite; a program needn't handle non-finite values.
Results may differ from a plain program's by a relative error of at most 0.0012.
Values may be sent and summed in bfloat16 or wider, within the bound.
No kernel may reach another device: no remote copies, remote signals or barrier semaphores. Data moves between devices by JAX's collectives and lax.ppermute only.
A program may use at most 192 MiB of HBM per device.

v0:
```python
import jax
import jax.numpy as jnp
from jax import lax
from jax.sharding import PartitionSpec as P

EPS = 1e-05


def per_device(
    hidden_states, norm_gain, head_weight, target_ids, loss_mask, seq_lengths, slot_order
):
    whole = lax.all_gather(hidden_states, "tensor", axis=1, tiled=True)
    values = whole.astype(jnp.float32)
    square = jnp.mean(values * values, axis=1, keepdims=True)
    normed = (values * lax.rsqrt(square + EPS) * norm_gain.astype(jnp.float32)).astype(jnp.bfloat16)
    rows = whole.shape[0]
    groups = lax.axis_size("tensor")
    share = rows // groups
    column_base = lax.axis_index("tensor") * (head_weight.shape[1] * lax.axis_size("dp"))
    piece = lax.all_gather(head_weight, "dp", axis=1, tiled=True)
    top = jnp.full((rows,), -1e30, jnp.float32)
    total = jnp.zeros((rows,), jnp.float32)
    logits = jnp.dot(normed, piece, preferred_element_type=jnp.float32)
    columns = column_base + lax.broadcasted_iota(jnp.int32, (1, piece.shape[1]), 1)
    new_top = jnp.maximum(top, jnp.max(logits, axis=1))
    shifted = logits - new_top[:, None]
    expo = jnp.exp(shifted)
    scale = jnp.exp(top - new_top)
    new_total = jnp.sum(expo, axis=1)
    new_spread = scale * (total * (top - new_top)) + jnp.sum(expo * shifted, axis=1)
    hit = jnp.sum(jnp.where(columns == target_ids[:, None], logits, 0.0), axis=1)
    mine = lax.axis_index("tensor") * share
    row_top = lax.pmax(new_top, "tensor")
    scale = jnp.exp(new_top - row_top)
    sums = lax.psum(
        (new_total * scale, scale * (new_spread + new_total * (new_top - row_top)), hit), "tensor"
    )
    row_top = lax.dynamic_slice_in_dim(row_top, mine, share)
    row_total = lax.dynamic_slice_in_dim(sums[0], mine, share)
    row_spread = lax.dynamic_slice_in_dim(sums[1], mine, share)
    row_picked = lax.dynamic_slice_in_dim(sums[2], mine, share)
    logsum = jnp.log(row_total)
    live = lax.dynamic_slice_in_dim(loss_mask, mine, share).astype(jnp.float32)
    token_logprob = (row_picked - row_top - logsum) * live
    token_entropy = (logsum - row_spread / row_total) * live
    ends = jnp.cumsum(seq_lengths)
    position = lax.axis_index("dp") * rows + mine + jnp.arange(share, dtype=jnp.int32)
    segment = jnp.sum((position[:, None] >= ends[None, :]).astype(jnp.int32), axis=1)
    member = (segment[:, None] == slot_order[None, :]).astype(jnp.float32)
    lp_part = jnp.dot(token_logprob, member, precision=lax.Precision.HIGHEST)
    ent_part = jnp.dot(token_entropy, member, precision=lax.Precision.HIGHEST)
    count_part = jnp.dot(live, member, precision=lax.Precision.HIGHEST)
    lp_sum, ent_sum, count = lax.psum((lp_part, ent_part, count_part), ("dp", "tensor"))
    owned = lp_sum.shape[0] // lax.axis_size("dp")
    first_slot = lax.axis_index("dp") * owned
    floor = jnp.maximum(lax.dynamic_slice_in_dim(count, first_slot, owned), 1.0)
    seq_mean_logprob = lax.dynamic_slice_in_dim(lp_sum, first_slot, owned) / floor
    seq_mean_entropy = lax.dynamic_slice_in_dim(ent_sum, first_slot, owned) / floor
    return (token_logprob, token_entropy, seq_mean_logprob, seq_mean_entropy)


def solution(mesh):
    placed = (P("dp", "tensor"), P(), P(None, ("tensor", "dp")), P("dp"), P("dp"), P(), P())
    return jax.shard_map(
        per_device,
        mesh=mesh,
        in_specs=placed,
        out_specs=(P(("dp", "tensor")), P(("dp", "tensor")), P("dp"), P("dp")),
        check_vma=False,
    )
```

profile of v0, /device:TPU:0, one launch (start us, length us, event | category | flops | bytes accessed | tf_op | source)
XLA Modules:
  0.0 416.9 jit_solution(15467861116896965682)
XLA Ops:
  7.2 0.0 all-gather.3.cloned.1.call-start
  7.2 0.7 all-gather.3.cloned.1.call-update
  7.9 0.0 all-gather.5.cloned.1.call-start
  7.9 0.7 all-gather.5.cloned.1.call-update
  8.7 0.7 convert_element_type.17
  9.3 0.7 copy.13
  10.1 0.1 reduce
  10.2 0.1 convert_reduce_fusion
  10.3 35.1 %all-gather.3.cloned.1.call-done = bf16[512,2048]{1,0:T(8,128)(2,1)} async-done(((bf16[512,1024]{1,0:T(8,128)(2,1)}), bf16[512,2048]{1,0:T(8,128)(2,1)}) %all-gather.3.cloned.1.call-update) | async-done | bytes 2097168 | tf_op jit(solution)/shard_map/all_gather | solution.py:12
  45.4 2.1 fusion.1
  47.5 256.5 %all-gather.5.cloned.1.call-done = bf16[2048,12800]{0,1:T(8,128)(2,1)} async-done(((bf16[2048,800]{0,1:T(8,128)(2,1)}), bf16[2048,12800]{0,1:T(8,128)(2,1)}) %all-gather.5.cloned.1.call-update) | async-done | bytes 52428816 | tf_op jit(solution)/shard_map/all_gather | solution.py:20
  304.0 35.8 %fusion.17 = (f32[512]{0:T(512)S(1)}, f32[512,12800]{1,0:T(8,128)}) fusion(bf16[2048,12800]{0,1:T(8,128)(2,1)} %all-gather.5.cloned.1.call-done, bf16[512,2048]{1,0:T(8,128)(2,1)} %all-gather.3.cloned.1.call-done, f32[2048]{0:T(1024)S(1)} %convert_element_type.17, f32[512]{0:T(512)S(1)} %add_rsqrt_fusion), kind=kOutput, calls=%fused_computation.34 | convolution fusion | flops 26854293504 | bytes 80752640 | tf_op jit(solution)/shard_map/dot_general | solution.py:23
  339.9 4.9 %pmax.7 = f32[512]{0:T(512)S(1)} all-reduce(f32[512]{0:T(512)S(1)} %broadcast_maximum_fusion), channel_id=1, replica_groups=mesh['dp'=16,'tensor'=2] {'tensor'}, use_global_device_ids=true, to_apply=%region_4.5 | all-reduce | flops 512 | bytes 4096 | tf_op jit(solution)/shard_map/pmax | solution.py:33
  344.8 13.5 %fusion = (f32[512]{0:T(512)S(1)}, f32[512]{0:T(512)S(1)}, f32[512]{0:T(512)S(1)}) fusion(f32[512,12800]{1,0:T(8,128)} %get-tuple-element.18, f32[512]{0:T(512)S(1)} %broadcast_maximum_fusion, s32[512]{0:T(512)S(1)} %copy-done, s32[12800]{0:T(1024)S(1)} %iota_add_fusion), kind=kLoop, calls=%fused_computation.2 | loop fusion | flops 45873664 | bytes 26275840 | tf_op jit(solution)/shard_map/reduce_sum | solution.py:30
  358.3 5.0 %all-reduce.1 = (f32[512]{0:T(512)S(1)}, f32[512]{0:T(512)S(1)}, f32[512]{0:T(512)S(1)}) all-reduce(f32[512]{0:T(512)S(1)} %get-tuple-element.6, f32[512]{0:T(512)S(1)} %get-tuple-element.16, f32[512]{0:T(512)S(1)} %get-tuple-element.15), channel_id=1, replica_groups=mesh['dp'=16,'tensor'=2] {'tensor'}, use_global_device_ids=true, to_apply=%region_2.0 | all-reduce | flops 1536 | bytes 12288 | tf_op jit(solution)/shard_map/psum | solution.py:35
  363.3 0.1 subtract_multiply_fusion
  363.4 0.2 convolution_bitcast_fusion
  363.6 0.2 convolution_bitcast_fusion.1
  363.9 0.1 subtract_multiply_fusion.1
  364.0 0.2 convolution_bitcast_fusion.2
  364.2 39.7 %all-reduce = (f32[16]{0:T(128)S(1)}, f32[16]{0:T(128)S(1)}, f32[16]{0:T(128)S(1)}) all-reduce(f32[16]{0:T(128)S(1)} %convolution_bitcast_fusion.2, f32[16]{0:T(128)S(1)} %convolution_bitcast_fusion.1, f32[16]{0:T(128)S(1)} %convolution_bitcast_fusion), channel_id=1, replica_groups=mesh['dp'=16,'tensor'=2] {'dp','tensor'}, use_global_device_ids=true, to_apply=%region_11.12 | all-reduce | flops 48 | bytes 384 | tf_op jit(solution)/shard_map/psum | solution.py:53
  403.9 0.7 dynamic_slice.31
  404.6 0.6 dynamic_slice.30
  405.2 0.6 dynamic_slice.29
  (16 shorter events, 0.1 us)
Async XLA Ops:
  7.2 38.3 %all-gather.3.cloned.1.call-start = ((), (), s32[]{:S(2)}) async-start(), calls=%async_computation | async-start | bytes 3145728 | tf_op jit(solution)/shard_map/all_gather | solution.py:12
  7.9 296.1 %all-gather.5.cloned.1.call-start = ((), (), s32[]{:S(2)}) async-start(), calls=%async_computation.1 | async-start | bytes 55705600 | tf_op jit(solution)/shard_map/all_gather | solution.py:20
  47.5 297.3 %copy-start = (s32[512]{0:T(512)S(1)}, s32[512]{0:T(512)}, u32[]{:S(2)}) copy-start(s32[512]{0:T(512)} %param.10) | copy-start | bytes 6148
  339.9 23.5 %copy-start.3 = (s32[512]{0:T(512)S(1)}, s32[512]{0:T(512)}, u32[]{:S(2)}) copy-start(s32[512]{0:T(512)} %param.11) | copy-start | bytes 6148
  339.9 23.6 %copy-start.4 = (s32[16]{0:T(128)S(1)}, s32[16]{0:T(128)}, u32[]{:S(2)}) copy-start(s32[16]{0:T(128)} %param.13) | copy-start | bytes 196
  363.4 44.3 %copy-start.1 = (f32[256]{0:T(256)}, f32[256]{0:T(256)S(1)}, u32[]{:S(2)}) copy-start(f32[256]{0:T(256)S(1)} %get-tuple-element.13) | copy-start | bytes 3076
  364.0 43.8 %copy-start.2 = (f32[256]{0:T(256)}, f32[256]{0:T(256)S(1)}, u32[]{:S(2)}) copy-start(f32[256]{0:T(256)S(1)} %subtract_multiply_fusion.1) | copy-start | bytes 3076
Sparse Core Ops, SparseCore 0:
  9.5 35.8 all-gather.2
  47.0 256.9 all-gather.4
where the time goes:
time: 417 us
  waiting for transfers between devices  293 us (70%)
  blocking collectives  49.7 us (12%)
  matrix products  36.5 us (9%)
  between operations  18.3 us (4%)
  other arithmetic  16.7 us (4%)
    all_gather x1, waiting for transfers between devices, per_device(): piece = lax.all_gather(head_weight, 'dp', axis=1, tiled=True)  257 us
    psum x1, blocking collectives, per_device(): lax.psum((lp_part, ent_part, count_part), ('dp', 'tensor'))  39.7 us
    dot_general x1, matrix products, per_device(): logits = jnp.dot(normed, piece, preferred_element_type=jnp.float32)  35.8 us
    all_gather x1, waiting for transfers between devices, per_device(): whole = lax.all_gather(hidden_states, 'tensor', axis=1, tiled=True)  35.1 us
    reduce_sum x1, other arithmetic, per_device(): jnp.sum(expo * shifted, axis=1)  13.5 us
  transfers between devices with their start and end apart: 2, of which 2 were waited for; matrix products, arithmetic and copies ran while one was open for 1% of the time, Pallas kernels for 0%

commit v1 on v0

--- a/solution.py
+++ b/solution.py
@@ -6,10 +6,32 @@
 EPS = 1e-05
 
 
+def joined_along(blocks, dim):
+    shape = list(blocks.shape[1:])
+    shape[dim] *= blocks.shape[0]
+    return jnp.moveaxis(blocks, 0, dim).reshape(shape)
+
+
+def grow_blocks(array, axis):
+    length = lax.axis_size(axis)
+    pieces = array[None]
+    for level in range(length.bit_length() - 1):
+        bit = 1 << level
+        other = lax.ppermute(pieces, axis, [(i, i ^ bit) for i in range(length)])
+        both = jnp.stack([pieces, other])
+        upper = lax.axis_index(axis) >> level & 1
+        pieces = jnp.where(upper == 0, both, both[::-1]).reshape(-1, *array.shape)
+    return pieces
+
+
+def gather_by_bits(x, axis, dim):
+    return joined_along(grow_blocks(x, axis), dim)
+
+
 def per_device(
     hidden_states, norm_gain, head_weight, target_ids, loss_mask, seq_lengths, slot_order
 ):
-    whole = lax.all_gather(hidden_states, "tensor", axis=1, tiled=True)
+    whole = gather_by_bits(hidden_states, "tensor", 1)
     values = whole.astype(jnp.float32)
     square = jnp.mean(values * values, axis=1, keepdims=True)
     normed = (values * lax.rsqrt(square + EPS) * norm_gain.astype(jnp.float32)).astype(jnp.bfloat16)

time: 417 us -> 382 us (0.916)
  waiting for transfers between devices: 293 us -> 255 us
    all_gather x1 -> x0, waiting for transfers between devices: 35.1 us -> none  [per_device(): whole = lax.all_gather(hidden_states, 'tensor', axis=1, tiled=True)]
    all_gather x1, waiting for transfers between devices: 257 us -> 232 us  [per_device(): piece = lax.all_gather(head_weight, 'dp', axis=1, tiled=True)]
    ppermute x0 -> x1, waiting for transfers between devices: none -> 22.8 us  [grow_blocks(): other = lax.ppermute(pieces, axis, [(i, i ^ bit) for i in range(length)])]
where the time goes in v1:
time: 382 us; the launch traced here: 381 us
  waiting for transfers between devices  255 us (67%)
  blocking collectives  49.6 us (13%)
  matrix products  35.7 us (9%)
  between operations  18.4 us (5%)
  other arithmetic  15.8 us (4%)
    all_gather x1, waiting for transfers between devices, per_device(): piece = lax.all_gather(head_weight, 'dp', axis=1, tiled=True)  232 us
    psum x1, blocking collectives, per_device(): lax.psum((lp_part, ent_part, count_part), ('dp', 'tensor'))  39.7 us
    dot_general x1, matrix products, per_device(): logits = jnp.dot(normed, piece, preferred_element_type=jnp.float32)  35 us
    ppermute x1, waiting for transfers between devices, grow_blocks(): other = lax.ppermute(pieces, axis, [(i, i ^ bit) for i in range(length)])  22.8 us
    reduce_sum x1, other arithmetic, per_device(): jnp.sum(expo * shifted, axis=1)  13.5 us
  transfers between devices with their start and end apart: 2, of which 2 were waited for; matrix products, arithmetic and copies ran while one was open for 1% of the time, Pallas kernels for 0%

profile of v1, /device:TPU:0, one launch (start us, length us, event | category | flops | bytes accessed | tf_op | source)
XLA Modules:
  0.0 381.3 jit_solution(14312540675489571394)
XLA Ops:
  7.2 0.7 all-gather.2.cloned.1.call-update
  7.9 1.5 copy.15
  9.4 3.0 collective-permute-start
  12.4 0.1 copy.17
  12.6 0.1 reduce.3
  12.7 0.1 convert_reduce_fusion
  12.8 22.8 %collective-permute-done = bf16[1,512,1024]{1,2,0:T(8,128)(2,1)S(1)} collective-permute-done((bf16[1,512,1024]{1,2,0:T(8,128)(2,1)S(1)}, bf16[1,512,1024]{1,2,0:T(8,128)(2,1)S(1)}, u32[]{:S(2)}, u32[]{:S(2)}) %collective-permute-start) | collective-permute-done | bytes 1048608 | tf_op jit(solution)/shard_map/ppermute | solution.py:20
  35.6 0.2 pad_maximum_fusion
  35.8 0.6 multiply_reduce_fusion
  36.4 0.6 fusion.3
  37.0 0.4 fusion.2
  37.5 231.9 %all-gather.2.cloned.1.call-done = bf16[2048,12800]{0,1:T(8,128)(2,1)} async-done(((bf16[2048,800]{0,1:T(8,128)(2,1)}), bf16[2048,12800]{0,1:T(8,128)(2,1)}) %all-gather.2.cloned.1.call-update) | async-done | bytes 52428816 | tf_op jit(solution)/shard_map/all_gather | solution.py:42
  269.3 35.0 %fusion.13 = (f32[512]{0:T(512)S(1)}, f32[512,12800]{1,0:T(8,128)}) fusion(bf16[512,2048]{0,1:T(8,128)(2,1)S(1)} %fusion.2, bf16[2048,12800]{0,1:T(8,128)(2,1)} %all-gather.2.cloned.1.call-done), kind=kOutput, calls=%fused_computation.33 | convolution fusion | flops 26850099200 | bytes 80742400 | tf_op jit(solution)/shard_map/dot_general | solution.py:45
  304.3 4.9 %pmax.7 = f32[512]{0:T(512)S(1)} all-reduce(f32[512]{0:T(512)S(1)} %broadcast_maximum_fusion), channel_id=1, replica_groups=mesh['dp'=16,'tensor'=2] {'tensor'}, use_global_device_ids=true, to_apply=%region_4.5 | all-reduce | flops 512 | bytes 4096 | tf_op jit(solution)/shard_map/pmax | solution.py:55
  309.3 13.5 %fusion = (f32[512]{0:T(512)S(1)}, f32[512]{0:T(512)S(1)}, f32[512]{0:T(512)S(1)}) fusion(f32[512,12800]{1,0:T(8,128)} %get-tuple-element.18, f32[512]{0:T(512)S(1)} %broadcast_maximum_fusion, s32[512]{0:T(512)S(1)} %copy-done.1, s32[12800]{0:T(1024)S(1)} %iota_add_fusion), kind=kLoop, calls=%fused_computation.2 | loop fusion | flops 45873664 | bytes 26275840 | tf_op jit(solution)/shard_map/reduce_sum | solution.py:52
  322.8 5.0 %all-reduce.1 = (f32[512]{0:T(512)S(1)}, f32[512]{0:T(512)S(1)}, f32[512]{0:T(512)S(1)}) all-reduce(f32[512]{0:T(512)S(1)} %get-tuple-element.6, f32[512]{0:T(512)S(1)} %get-tuple-element.16, f32[512]{0:T(512)S(1)} %get-tuple-element.15), channel_id=1, replica_groups=mesh['dp'=16,'tensor'=2] {'tensor'}, use_global_device_ids=true, to_apply=%region_2.3 | all-reduce | flops 1536 | bytes 12288 | tf_op jit(solution)/shard_map/psum | solution.py:57
  327.9 0.2 convolution_bitcast_fusion
  328.1 0.2 convolution_bitcast_fusion.1
  328.4 0.1 subtract_multiply_fusion.1
  328.4 0.2 convolution_bitcast_fusion.2
  328.7 39.7 %all-reduce = (f32[16]{0:T(128)S(1)}, f32[16]{0:T(128)S(1)}, f32[16]{0:T(128)S(1)}) all-reduce(f32[16]{0:T(128)S(1)} %convolution_bitcast_fusion.2, f32[16]{0:T(128)S(1)} %convolution_bitcast_fusion.1, f32[16]{0:T(128)S(1)} %convolution_bitcast_fusion), channel_id=1, replica_groups=mesh['dp'=16,'tensor'=2] {'dp','tensor'}, use_global_device_ids=true, to_apply=%region_11.12 | all-reduce | flops 48 | bytes 384 | tf_op jit(solution)/shard_map/psum | solution.py:75
  368.4 0.7 dynamic_slice.31
  369.0 0.6 dynamic_slice.30
  369.6 0.6 dynamic_slice.29
  (23 shorter events, 0.2 us)
Async XLA Ops:
  7.2 5.3 %copy-start = (bf16[2048]{0:T(1024)(128)(2,1)S(1)}, bf16[2048]{0:T(1024)(128)(2,1)}, u32[]{:S(2)}) copy-start(bf16[2048]{0:T(1024)(128)(2,1)} %param.8) | copy-start | bytes 12292
  7.2 5.3 %copy-start.4 = (s32[16]{0:T(128)S(1)}, s32[16]{0:T(128)}, u32[]{:S(2)}) copy-start(s32[16]{0:T(128)} %param.12) | copy-start | bytes 196
  7.2 262.1 %all-gather.2.cloned.1.call-start = ((), (), s32[]{:S(2)}) async-start(), calls=%async_computation | async-start | bytes 55705600 | tf_op jit(solution)/shard_map/all_gather | solution.py:42
  9.4 26.2 %collective-permute-start = (bf16[1,512,1024]{1,2,0:T(8,128)(2,1)S(1)}, bf16[1,512,1024]{1,2,0:T(8,128)(2,1)S(1)}, u32[]{:S(2)}, u32[]{:S(2)}) collective-permute-start(bf16[1,512,1024]{1,2,0:T(8,128)(2,1)S(1)} %bitcast.28), channel_id=1, source_target_pairs={{0,1},{1,0},{2,3},{3,2},{4,5},{5,4},{6,7},{7,6},{8,9},{9,8},{10,11... | collective-permute-start | bytes 3145736 | tf_op jit(solution)/shard_map/ppermute | solution.py:20
  37.4 271.8 %copy-start.1 = (s32[512]{0:T(512)S(1)}, s32[512]{0:T(512)}, u32[]{:S(2)}) copy-start(s32[512]{0:T(512)} %param.10) | copy-start | bytes 6148
  309.3 18.5 %copy-start.5 = (s32[512]{0:T(512)S(1)}, s32[512]{0:T(512)}, u32[]{:S(2)}) copy-start(s32[512]{0:T(512)} %param.11) | copy-start | bytes 6148
  309.3 18.6 %copy-start.6 = (s32[16]{0:T(128)S(1)}, s32[16]{0:T(128)}, u32[]{:S(2)}) copy-start(s32[16]{0:T(128)} %param.13) | copy-start | bytes 196
  327.9 44.3 %copy-start.2 = (f32[256]{0:T(256)}, f32[256]{0:T(256)S(1)}, u32[]{:S(2)}) copy-start(f32[256]{0:T(256)S(1)} %get-tuple-element.13) | copy-start | bytes 3076
  328.4 43.8 %copy-start.3 = (f32[256]{0:T(256)}, f32[256]{0:T(256)S(1)}, u32[]{:S(2)}) copy-start(f32[256]{0:T(256)S(1)} %subtract_multiply_fusion.1) | copy-start | bytes 3076
Sparse Core Ops, SparseCore 0:
  9.6 259.6 all-gather.1
